TPU v7x, 512 devices: a whole 4x8x8 slice. The times are simulated.
512 devices in a mesh: az: 64 (over z, y_lo, core), rad: 8 (over y_hi, x).
Axes of the slice: x: 4, y: 8 (y_hi: 2, y_lo: 4; y = y_hi * 4 + y_lo), z: 8, core: 2. Of those that a mesh axis runs over, the one named last changes fastest.
Arguments:
- density: float32 [1024, 384, 128], P('az', 'rad'), may hold values from 0.5 to 1.5
- flow_vars: float32 [4, 1024, 384, 128], P(None, 'az', 'rad'), may hold values from -6 to 6
- blade_offset: int32 [4], replicated, may hold values from 0 to 4, as said below
- smooth_width: int32 [128], replicated, may hold values from 1 to 4, as said below
Outputs:
- mean_fields: float32 [5, 1024, 384, 128], P(None, 'az', 'rad')
- q_field: float32 [1024, 384, 128], P('az', 'rad')
Inputs may be any that keep to these rules, and one draw needn't show every extreme that they name: `blade_offset`: some blade's passage has the offset 4. `smooth_width`: some axial station uses the half-width 4.
All inputs are finite; a program needn't handle non-finite values.
Results may differ from a plain program's by a relative error of at most 0.00002.
Values sent between devices are 32-bit elements; how exact they have to be, the bound alone decides.
No kernel may reach another device: no remote copies, remote signals or barrier semaphores. Data moves between devices by JAX's collectives and lax.ppermute only.
A program may use at most 64 MiB of HBM per device.

v0:
```python
import math
import jax
import jax.numpy as jnp
from jax import lax
from jax.sharding import PartitionSpec as P

BLADES = 4
MAXOFF = 4
HW = 4
AZ = ("blade", "slab")


def passed_along(block, axis, distance):
    devices = range(lax.axis_size(axis))
    route = [((i - distance) % len(devices), i) for i in devices]
    return lax.ppermute(block, axis, route)


def extended(block, sides, width, periodic):
    for axis, dim in sides:
        count = lax.axis_size(axis)
        forward = [(i, i + 1) for i in range(count - 1)]
        if periodic:
            forward.append((count - 1, 0))
        backward = [(target, source) for source, target in forward]
        low = lax.ppermute(
            lax.slice_in_dim(block, block.shape[dim] - width, None, axis=dim), axis, forward
        )
        high = lax.ppermute(lax.slice_in_dim(block, 0, width, axis=dim), axis, backward)
        block = jnp.concatenate([low, block, high], axis=dim)
    return block


def smoothing_taps(smooth_width):
    spread = jnp.arange(-HW, HW + 1)
    width = smooth_width.astype(jnp.float32)
    square = (spread.astype(jnp.float32) ** 2)[:, None]
    weights = jnp.where(
        jnp.abs(spread)[:, None] <= smooth_width[None, :],
        jnp.exp(-0.5 * square / (width * width)[None, :]),
        0.0,
    )
    return weights / jnp.sum(weights, axis=0, keepdims=True)


def apply_taps(source, taps, length):
    total = jnp.zeros(source.shape[:1] + (length,) + source.shape[2:], jnp.float32)
    for turn in range(2 * HW + 1):
        total = total + taps[turn] * source[:, turn : turn + length]
    return total


def edge_rate(field, axis):
    count = field.shape[axis]
    upper = jnp.concatenate(
        [
            lax.slice_in_dim(field, 1, count, axis=axis),
            lax.slice_in_dim(field, count - 1, count, axis=axis),
        ],
        axis=axis,
    )
    lower = jnp.concatenate(
        [
            lax.slice_in_dim(field, 0, 1, axis=axis),
            lax.slice_in_dim(field, 0, count - 1, axis=axis),
        ],
        axis=axis,
    )
    places = jnp.arange(count)
    span = jnp.where((places == 0) | (places == count - 1), 1.0, 2.0).astype(field.dtype)
    layout = [1] * field.ndim
    layout[axis] = count
    return (upper - lower) / span.reshape(layout)


def swirl_measure(smoothed, az_rate, radial_rate, axial_rate, radius):
    tensor_aa = radial_rate[0]
    tensor_ab = (az_rate[0] - smoothed[1]) / radius
    tensor_ac = axial_rate[0]
    tensor_ba = radial_rate[1]
    tensor_bb = (az_rate[1] + smoothed[0]) / radius
    tensor_bc = axial_rate[1]
    tensor_ca = radial_rate[2]
    tensor_cb = az_rate[2] / radius
    tensor_cc = axial_rate[2]
    diagonal_part = tensor_aa * tensor_aa + tensor_bb * tensor_bb + tensor_cc * tensor_cc
    cross_part = tensor_ab * tensor_ba + tensor_ac * tensor_ca + tensor_bc * tensor_cb
    return -0.5 * (diagonal_part + 2.0 * cross_part)


def shards(density, flow_vars, blade_offset, smooth_width):
    cells = density.shape[0]
    rad_cells = density.shape[1]
    group = lax.axis_size("slab")
    blade = lax.axis_index("blade")
    own_offset = jnp.sum(jnp.where(jnp.arange(BLADES) == blade, blade_offset, 0))
    velocity = flow_vars[0:3]
    carried = jnp.concatenate([density[None], density[None] * velocity, flow_vars[3:4]], axis=0)
    ahead = passed_along(carried[:, :MAXOFF], AZ, -1)
    contribution = lax.dynamic_slice_in_dim(
        jnp.concatenate([carried, ahead], axis=1), own_offset, cells, 1
    )
    sector_part = lax.psum(contribution, "blade")
    behind = passed_along(sector_part[:, cells - MAXOFF :], AZ, 1)
    phase_sums = lax.dynamic_slice_in_dim(
        jnp.concatenate([behind, sector_part], axis=1), MAXOFF - own_offset, cells, 1
    )
    mean_fields = jnp.concatenate(
        [phase_sums[0:1] / BLADES, phase_sums[1:4] / phase_sums[0:1], phase_sums[4:5] / BLADES],
        axis=0,
    )
    fluctuation = velocity - mean_fields[1:4]
    taps = smoothing_taps(smooth_width)
    rimmed = extended(fluctuation, ((AZ, 1),), HW, True)
    smoothed = apply_taps(rimmed, taps, cells)
    az_side = extended(smoothed, ((AZ, 1),), 1, True)
    rad_side = extended(smoothed, (("rad", 2),), 1, False)
    dtheta = 2.0 * math.pi / (cells * lax.axis_size(AZ))
    az_rate = (az_side[:, 2:] - az_side[:, :-2]) / (2.0 * dtheta)
    total_rad = rad_cells * lax.axis_size("rad")
    rows = lax.axis_index("rad") * rad_cells + jnp.arange(rad_cells)
    upper = jnp.where((rows == total_rad - 1)[:, None], smoothed, rad_side[:, :, 2:])
    lower = jnp.where((rows == 0)[:, None], smoothed, rad_side[:, :, :-2])
    span = jnp.where((rows == 0) | (rows == total_rad - 1), 1.0, 2.0).astype(jnp.float32)
    radial_rate = (upper - lower) / span[:, None]
    axial_rate = edge_rate(smoothed, 3)
    radius = (total_rad / 2 + rows.astype(jnp.float32) + 0.5)[:, None]
    q_field = swirl_measure(smoothed, az_rate, radial_rate, axial_rate, radius)
    return (mean_fields, q_field)


def solution(mesh):
    az, rad = mesh.devices.shape
    split = jax.sharding.Mesh(
        mesh.devices.reshape(BLADES, az // BLADES, rad), ("blade", "slab", "rad")
    )
    in_specs = (P(AZ, "rad", None), P(None, AZ, "rad", None), P(), P())
    out_specs = (P(None, AZ, "rad", None), P(AZ, "rad", None))
    return jax.shard_map(
        shards, mesh=split, in_specs=in_specs, out_specs=out_specs, check_vma=False
    )
```

profile of v0, /device:TPU:32, one launch (start us, length us, event | category | flops | bytes accessed | tf_op | source)
XLA Modules:
  0.0 195.5 jit_solution(17805172556178679589)
XLA Ops:
  7.2 1.0 slice.161
  8.2 1.5 slice_multiply_fusion
  9.8 10.7 %collective-permute-start = (f32[5,4,48,128]{3,2,1,0:T(8,128)S(1)}, f32[5,4,48,128]{3,2,1,0:T(8,128)S(1)}, u32[]{:S(2)}, u32[]{:S(2)}) collective-permute-start(f32[5,4,48,128]{3,2,1,0:T(8,128)S(1)} %pad_maximum_fusion.7), channel_id=1, source_target_pairs={{8,0},{16,8},{24,16},{32,24},{40,32},{48,40},{56,48},{64,56},{72,6... | collective-permute-start | bytes 1474568 | tf_op jit(solution)/shard_map/ppermute | solution.py:16
  20.6 0.6 fusion.54
  23.1 3.7 %collective-permute-done = f32[5,4,48,128]{3,2,1,0:T(8,128)S(1)} collective-permute-done((f32[5,4,48,128]{3,2,1,0:T(8,128)S(1)}, f32[5,4,48,128]{3,2,1,0:T(8,128)S(1)}, u32[]{:S(2)}, u32[]{:S(2)}) %collective-permute-start) | collective-permute-done | bytes 491552 | tf_op jit(solution)/shard_map/ppermute | solution.py:16
  26.9 1.5 fusion.3
  28.5 0.6 copy-done.2
  29.1 0.1 fusion.53
  29.2 98.0 %all-reduce.2.cloned.1.call-done = f32[5,16,48,128]{3,2,1,0:T(8,128)} async-done(((f32[5,16,48,128]{3,2,1,0:T(8,128)}), f32[5,16,48,128]{3,2,1,0:T(8,128)}) %all-reduce.2.cloned.1.call-update) | async-done | bytes 1966096 | tf_op jit(solution)/shard_map/psum | solution.py:103
  127.1 1.1 slice.209
  128.2 1.9 collective-permute-start.1
  131.5 10.7 %collective-permute-done.1 = f32[5,4,48,128]{3,2,1,0:T(8,128)S(1)} collective-permute-done((f32[5,4,48,128]{3,2,1,0:T(8,128)S(1)}, f32[5,4,48,128]{3,2,1,0:T(8,128)S(1)}, u32[]{:S(2)}, u32[]{:S(2)}) %collective-permute-start.1) | collective-permute-done | bytes 491552 | tf_op jit(solution)/shard_map/ppermute | solution.py:16
  142.3 1.6 fusion
  143.8 0.1 slice_multiply_fusion.5
  143.9 1.3 copy-done
  145.2 0.3 slice_subtract_fusion
  145.6 1.9 collective-permute-start.2
  147.5 7.5 %collective-permute-start.3 = (f32[3,4,48,128]{3,2,1,0:T(8,128)S(1)}, f32[3,4,48,128]{3,2,1,0:T(8,128)S(1)}, u32[]{:S(2)}, u32[]{:S(2)}) collective-permute-start(f32[3,4,48,128]{3,2,1,0:T(8,128)S(1)} %get-tuple-element.18), channel_id=1, source_target_pairs={{8,0},{16,8},{24,16},{32,24},{40,32},{48,40},{56,48},{64,56},{72,6... | collective-permute-start | bytes 884744 | tf_op jit(solution)/shard_map/ppermute | solution.py:29
  155.1 1.5 pad_maximum_fusion
  156.5 1.6 collective-permute-done.2
  158.2 1.1 collective-permute-done.3
  159.3 1.1 fusion.7
  160.4 0.4 fusion.59
  160.8 0.4 fusion.60
  161.2 7.7 %collective-permute-start.6 = (f32[3,1,48,128]{3,2,1,0:T(8,128)S(1)}, f32[3,1,48,128]{3,2,1,0:T(8,128)S(1)}, u32[]{:S(2)}, u32[]{:S(2)}) collective-permute-start(f32[3,1,48,128]{3,2,1,0:T(8,128)S(1)} %get-tuple-element.15), channel_id=1, source_target_pairs={{8,0},{16,8},{24,16},{32,24},{40,32},{48,40},{56,48},{64,56},{72,6... | collective-permute-start | bytes 221192 | tf_op jit(solution)/shard_map/ppermute | solution.py:29
  168.9 1.9 collective-permute-start.7
  170.9 4.5 %collective-permute-start.4 = (f32[3,16,1,128]{3,2,1,0:T(1,128)S(1)}, f32[3,16,1,128]{3,2,1,0:T(1,128)S(1)}, u32[]{:S(2)}, u32[]{:S(2)}) collective-permute-start(f32[3,16,1,128]{3,2,1,0:T(1,128)S(1)} %get-tuple-element.9), channel_id=1, source_target_pairs={{1,0},{2,1},{3,2},{4,3},{5,4},{6,5},{7,6},{9,8},{10,9},{11,10},{12... | collective-permute-start | bytes 73736 | tf_op jit(solution)/shard_map/ppermute | solution.py:29
  175.4 1.9 collective-permute-start.5
  177.3 0.7 fusion.32
  178.0 9.1 %collective-permute-done.5 = f32[3,16,1,128]{3,2,1,0:T(1,128)S(1)} collective-permute-done((f32[3,16,1,128]{3,2,1,0:T(1,128)S(1)}, f32[3,16,1,128]{3,2,1,0:T(1,128)S(1)}, u32[]{:S(2)}, u32[]{:S(2)}) %collective-permute-start.5) | collective-permute-done | bytes 24608 | tf_op jit(solution)/shard_map/ppermute | solution.py:26
  187.1 0.5 fusion.28
  187.6 1.1 fusion.38
  (23 shorter events, 0.3 us)
Async XLA Ops:
  7.2 120.0 %all-reduce.2.cloned.1.call-start = ((), (), s32[]{:S(2)}) async-start(), calls=%async_computation | async-start | bytes 3932160 | tf_op jit(solution)/shard_map/psum | solution.py:103
  8.2 1.5 copy-start.1
  9.8 10.8 %copy-start.3 = (s32[4]{0:T(128)S(1)}, s32[4]{0:T(128)}, u32[]{:S(2)}) copy-start(s32[4]{0:T(128)} %param.6) | copy-start | bytes 52
  9.8 17.1 %collective-permute-start = (f32[5,4,48,128]{3,2,1,0:T(8,128)S(1)}, f32[5,4,48,128]{3,2,1,0:T(8,128)S(1)}, u32[]{:S(2)}, u32[]{:S(2)}) collective-permute-start(f32[5,4,48,128]{3,2,1,0:T(8,128)S(1)} %pad_maximum_fusion.7), channel_id=1, source_target_pairs={{8,0},{16,8},{24,16},{32,24},{40,32},{48,40},{56,48},{64,56},{72,6... | collective-permute-start | bytes 1474568 | tf_op jit(solution)/shard_map/ppermute | solution.py:16
  28.4 0.7 copy-start.2
  128.2 14.1 %collective-permute-start.1 = (f32[5,4,48,128]{3,2,1,0:T(8,128)S(1)}, f32[5,4,48,128]{3,2,1,0:T(8,128)S(1)}, u32[]{:S(2)}, u32[]{:S(2)}) collective-permute-start(f32[5,4,48,128]{3,2,1,0:T(8,128)S(1)} %slice.209), channel_id=1, source_target_pairs={{504,0},{0,8},{8,16},{16,24},{24,32},{32,40},{40,48},{48,56},{56,6... | collective-permute-start | bytes 1474568 | tf_op jit(solution)/shard_map/ppermute | solution.py:16
  143.8 1.4 copy-start
  145.6 12.6 %collective-permute-start.2 = (f32[3,4,48,128]{3,2,1,0:T(8,128)S(1)}, f32[3,4,48,128]{3,2,1,0:T(8,128)S(1)}, u32[]{:S(2)}, u32[]{:S(2)}) collective-permute-start(f32[3,4,48,128]{3,2,1,0:T(8,128)S(1)} %get-tuple-element.17), channel_id=1, source_target_pairs={{0,8},{8,16},{16,24},{24,32},{32,40},{40,48},{48,56},{56,64},{64,7... | collective-permute-start | bytes 884744 | tf_op jit(solution)/shard_map/ppermute | solution.py:26
  147.5 11.8 %collective-permute-start.3 = (f32[3,4,48,128]{3,2,1,0:T(8,128)S(1)}, f32[3,4,48,128]{3,2,1,0:T(8,128)S(1)}, u32[]{:S(2)}, u32[]{:S(2)}) collective-permute-start(f32[3,4,48,128]{3,2,1,0:T(8,128)S(1)} %get-tuple-element.18), channel_id=1, source_target_pairs={{8,0},{16,8},{24,16},{32,24},{40,32},{48,40},{56,48},{64,56},{72,6... | collective-permute-start | bytes 884744 | tf_op jit(solution)/shard_map/ppermute | solution.py:29
  161.2 25.9 %collective-permute-start.6 = (f32[3,1,48,128]{3,2,1,0:T(8,128)S(1)}, f32[3,1,48,128]{3,2,1,0:T(8,128)S(1)}, u32[]{:S(2)}, u32[]{:S(2)}) collective-permute-start(f32[3,1,48,128]{3,2,1,0:T(8,128)S(1)} %get-tuple-element.15), channel_id=1, source_target_pairs={{8,0},{16,8},{24,16},{32,24},{40,32},{48,40},{56,48},{64,56},{72,6... | collective-permute-start | bytes 221192 | tf_op jit(solution)/shard_map/ppermute | solution.py:29
  168.9 18.2 %collective-permute-start.7 = (f32[3,1,48,128]{3,2,1,0:T(8,128)S(1)}, f32[3,1,48,128]{3,2,1,0:T(8,128)S(1)}, u32[]{:S(2)}, u32[]{:S(2)}) collective-permute-start(f32[3,1,48,128]{3,2,1,0:T(8,128)S(1)} %get-tuple-element.16), channel_id=1, source_target_pairs={{0,8},{8,16},{16,24},{24,32},{32,40},{40,48},{48,56},{56,64},{64,7... | collective-permute-start | bytes 221192 | tf_op jit(solution)/shard_map/ppermute | solution.py:26
  170.9 7.1 %collective-permute-start.4 = (f32[3,16,1,128]{3,2,1,0:T(1,128)S(1)}, f32[3,16,1,128]{3,2,1,0:T(1,128)S(1)}, u32[]{:S(2)}, u32[]{:S(2)}) collective-permute-start(f32[3,16,1,128]{3,2,1,0:T(1,128)S(1)} %get-tuple-element.9), channel_id=1, source_target_pairs={{1,0},{2,1},{3,2},{4,3},{5,4},{6,5},{7,6},{9,8},{10,9},{11,10},{12... | collective-permute-start | bytes 73736 | tf_op jit(solution)/shard_map/ppermute | solution.py:29
  175.4 11.7 %collective-permute-start.5 = (f32[3,16,1,128]{3,2,1,0:T(1,128)S(1)}, f32[3,16,1,128]{3,2,1,0:T(1,128)S(1)}, u32[]{:S(2)}, u32[]{:S(2)}) collective-permute-start(f32[3,16,1,128]{3,2,1,0:T(1,128)S(1)} %get-tuple-element.10), channel_id=1, source_target_pairs={{0,1},{1,2},{2,3},{3,4},{4,5},{5,6},{6,7},{8,9},{9,10},{10,11},{11... | collective-permute-start | bytes 73736 | tf_op jit(solution)/shard_map/ppermute | solution.py:26
Sparse Core Ops, SparseCore 0:
  28.6 98.5 all-reduce.1
where the time goes:
time: 196 us; the launch traced here: 195 us
  waiting for transfers between devices  124 us (63%)
  starting transfers between devices  38.2 us (19%)
  between operations  17.5 us (9%)
  other arithmetic  10.6 us (5%)
  local copies, waits for them, and re-layouts  4.86 us (2%)
    psum x1, waiting for transfers between devices, shards(): sector_part = lax.psum(contribution, 'blade')  98 us
    ppermute x3, starting transfers between devices, extended(): lax.ppermute(lax.slice_in_dim(block, 0, width, axis=dim), axis, backward)  19.8 us
    ppermute x2, waiting for transfers between devices, passed_along(): return lax.ppermute(block, axis, route)  14.5 us
    ppermute x2, starting transfers between devices, passed_along(): return lax.ppermute(block, axis, route)  12.6 us
    ppermute x3, waiting for transfers between devices, extended(): lax.ppermute(lax.slice_in_dim(block, block.shape[dim] - width, None, axis...  10.8 us
    ppermute x3, starting transfers between devices, extended(): lax.ppermute(lax.slice_in_dim(block, block.shape[dim] - width, None, axis...  5.76 us
  transfers between devices with their start and end apart: 9, of which 6 were waited for; matrix products, arithmetic and copies ran while one was open for 2% of the time, Pallas kernels for 0%

commit v1 on v0

--- a/solution.py
+++ b/solution.py
@@ -100,7 +100,7 @@
     contribution = lax.dynamic_slice_in_dim(
         jnp.concatenate([carried, ahead], axis=1), own_offset, cells, 1
     )
-    sector_part = lax.psum(contribution, "blade")
+    sector_part = jnp.sum(lax.all_gather(contribution, "blade"), axis=0)
     behind = passed_along(sector_part[:, cells - MAXOFF :], AZ, 1)
     phase_sums = lax.dynamic_slice_in_dim(
         jnp.concatenate([behind, sector_part], axis=1), MAXOFF - own_offset, cells, 1

time: 196 us -> 247 us (1.26)
  waiting for transfers between devices: 124 us -> 174 us
  other arithmetic: 10.6 us -> 13.3 us
    all_gather x0 -> x1, waiting for transfers between devices: none -> 148 us  [shards(): sector_part = jnp.sum(lax.all_gather(contribution, 'blade'), axis=0)]
    psum x1 -> x0, waiting for transfers between devices: 98 us -> none  [shards(): sector_part = lax.psum(contribution, 'blade')]
    reduce_sum x0 -> x1, other arithmetic: none -> 3.97 us  [shards(): sector_part = jnp.sum(lax.all_gather(contribution, 'blade'), axis=0)]
  transfers between devices with their start and end apart: 9 -> 9, of which waited for: 6 -> 6; matrix products, arithmetic and copies ran while one was open for 2% -> 1% of each run, Pallas kernels for 0% -> 0%
where the time goes in v1:
time: 247 us
  waiting for transfers between devices  174 us (70%)
  starting transfers between devices  38.2 us (15%)
  between operations  17.5 us (7%)
  other arithmetic  13.3 us (5%)
  local copies, waits for them, and re-layouts  3.83 us (2%)
    all_gather x1, waiting for transfers between devices, shards(): sector_part = jnp.sum(lax.all_gather(contribution, 'blade'), axis=0)  148 us
    ppermute x3, starting transfers between devices, extended(): lax.ppermute(lax.slice_in_dim(block, 0, width, axis=dim), axis, backward)  19.8 us
    ppermute x2, waiting for transfers between devices, passed_along(): return lax.ppermute(block, axis, route)  14.5 us
    ppermute x2, starting transfers between devices, passed_along(): return lax.ppermute(block, axis, route)  12.6 us
    ppermute x3, waiting for transfers between devices, extended(): lax.ppermute(lax.slice_in_dim(block, block.shape[dim] - width, None, axis...  9.98 us
    ppermute x3, starting transfers between devices, extended(): lax.ppermute(lax.slice_in_dim(block, block.shape[dim] - width, None, axis...  5.76 us
  transfers between devices with their start and end apart: 9, of which 6 were waited for; matrix products, arithmetic and copies ran while one was open for 1% of the time, Pallas kernels for 0%

profile of v1, /device:TPU:32, one launch (start us, length us, event | category | flops | bytes accessed | tf_op | source)
XLA Modules:
  0.0 246.9 jit_solution(18016781431365652815)
XLA Ops:
  7.2 1.0 slice.161
  8.2 1.5 slice_multiply_fusion
  9.8 10.7 %collective-permute-start = (f32[5,4,48,128]{3,2,1,0:T(8,128)S(1)}, f32[5,4,48,128]{3,2,1,0:T(8,128)S(1)}, u32[]{:S(2)}, u32[]{:S(2)}) collective-permute-start(f32[5,4,48,128]{3,2,1,0:T(8,128)S(1)} %pad_maximum_fusion.7), channel_id=1, source_target_pairs={{8,0},{16,8},{24,16},{32,24},{40,32},{48,40},{56,48},{64,56},{72,6... | collective-permute-start | bytes 1474568 | tf_op jit(solution)/shard_map/ppermute | solution.py:16
  20.6 0.6 fusion.54
  23.1 3.7 %collective-permute-done = f32[5,4,48,128]{3,2,1,0:T(8,128)S(1)} collective-permute-done((f32[5,4,48,128]{3,2,1,0:T(8,128)S(1)}, f32[5,4,48,128]{3,2,1,0:T(8,128)S(1)}, u32[]{:S(2)}, u32[]{:S(2)}) %collective-permute-start) | collective-permute-done | bytes 491552 | tf_op jit(solution)/shard_map/ppermute | solution.py:16
  26.9 1.5 fusion.3
  28.5 0.6 copy-done.2
  29.1 0.1 fusion.53
  29.2 147.7 %all-gather.3.cloned.1.call-done = f32[20,16,48,128]{3,2,1,0:T(8,128)} async-done(((f32[5,16,48,128]{3,2,1,0:T(8,128)}), f32[20,16,48,128]{3,2,1,0:T(8,128)}) %all-gather.3.cloned.1.call-update) | async-done | bytes 7864336 | tf_op jit(solution)/shard_map/all_gather | solution.py:103
  176.9 4.0 %reduce_sum.28 = f32[5,16,48,128]{3,2,1,0:T(8,128)S(1)} reduce(f32[4,5,16,48,128]{4,3,2,1,0:T(8,128)} %bitcast.78, f32[]{:T(128)} %constant.21.clone.1), dimensions={0}, to_apply=%region_1.2 | reduce | flops 1474560 | bytes 9830404 | tf_op jit(solution)/shard_map/reduce_sum | solution.py:103
  180.9 1.9 collective-permute-start.1
  184.2 10.7 %collective-permute-done.1 = f32[5,4,48,128]{3,2,1,0:T(8,128)S(1)} collective-permute-done((f32[5,4,48,128]{3,2,1,0:T(8,128)S(1)}, f32[5,4,48,128]{3,2,1,0:T(8,128)S(1)}, u32[]{:S(2)}, u32[]{:S(2)}) %collective-permute-start.1) | collective-permute-done | bytes 491552 | tf_op jit(solution)/shard_map/ppermute | solution.py:16
  195.0 0.2 fusion
  195.2 0.1 slice_multiply_fusion.5
  195.3 1.3 copy-done
  196.6 0.3 slice_subtract_fusion
  196.9 1.9 collective-permute-start.2
  198.9 7.5 %collective-permute-start.3 = (f32[3,4,48,128]{3,2,1,0:T(8,128)S(1)}, f32[3,4,48,128]{3,2,1,0:T(8,128)S(1)}, u32[]{:S(2)}, u32[]{:S(2)}) collective-permute-start(f32[3,4,48,128]{3,2,1,0:T(8,128)S(1)} %get-tuple-element.18), channel_id=1, source_target_pairs={{8,0},{16,8},{24,16},{32,24},{40,32},{48,40},{56,48},{64,56},{72,6... | collective-permute-start | bytes 884744 | tf_op jit(solution)/shard_map/ppermute | solution.py:29
  206.4 1.5 pad_maximum_fusion
  207.9 1.0 collective-permute-done.2
  208.9 1.8 collective-permute-done.3
  210.6 1.1 fusion.7
  211.7 0.4 fusion.59
  212.1 0.4 fusion.60
  212.6 7.8 %collective-permute-start.6 = (f32[3,1,48,128]{3,2,1,0:T(8,128)S(1)}, f32[3,1,48,128]{3,2,1,0:T(8,128)S(1)}, u32[]{:S(2)}, u32[]{:S(2)}) collective-permute-start(f32[3,1,48,128]{3,2,1,0:T(8,128)S(1)} %get-tuple-element.15), channel_id=1, source_target_pairs={{8,0},{16,8},{24,16},{32,24},{40,32},{48,40},{56,48},{64,56},{72,6... | collective-permute-start | bytes 221192 | tf_op jit(solution)/shard_map/ppermute | solution.py:29
  220.3 1.9 collective-permute-start.7
  222.3 4.5 %collective-permute-start.4 = (f32[3,16,1,128]{3,2,1,0:T(1,128)S(1)}, f32[3,16,1,128]{3,2,1,0:T(1,128)S(1)}, u32[]{:S(2)}, u32[]{:S(2)}) collective-permute-start(f32[3,16,1,128]{3,2,1,0:T(1,128)S(1)} %get-tuple-element.9), channel_id=1, source_target_pairs={{1,0},{2,1},{3,2},{4,3},{5,4},{6,5},{7,6},{9,8},{10,9},{11,10},{12... | collective-permute-start | bytes 73736 | tf_op jit(solution)/shard_map/ppermute | solution.py:29
  226.7 1.9 collective-permute-start.5
  228.7 0.8 fusion.32
  229.5 9.0 %collective-permute-done.5 = f32[3,16,1,128]{3,2,1,0:T(1,128)S(1)} collective-permute-done((f32[3,16,1,128]{3,2,1,0:T(1,128)S(1)}, f32[3,16,1,128]{3,2,1,0:T(1,128)S(1)}, u32[]{:S(2)}, u32[]{:S(2)}) %collective-permute-start.5) | collective-permute-done | bytes 24608 | tf_op jit(solution)/shard_map/ppermute | solution.py:26
  238.5 0.5 fusion.28
  239.0 1.1 fusion.38
  (24 shorter events, 0.4 us)
Async XLA Ops:
  7.2 169.7 %all-gather.3.cloned.1.call-start = ((), (), s32[]{:S(2)}) async-start(), calls=%async_computation | async-start | bytes 9830400 | tf_op jit(solution)/shard_map/all_gather | solution.py:103
  8.2 1.5 copy-start.1
  9.8 10.8 %copy-start.3 = (s32[4]{0:T(128)S(1)}, s32[4]{0:T(128)}, u32[]{:S(2)}) copy-start(s32[4]{0:T(128)} %param.6) | copy-start | bytes 52
  9.8 17.1 %collective-permute-start = (f32[5,4,48,128]{3,2,1,0:T(8,128)S(1)}, f32[5,4,48,128]{3,2,1,0:T(8,128)S(1)}, u32[]{:S(2)}, u32[]{:S(2)}) collective-permute-start(f32[5,4,48,128]{3,2,1,0:T(8,128)S(1)} %pad_maximum_fusion.7), channel_id=1, source_target_pairs={{8,0},{16,8},{24,16},{32,24},{40,32},{48,40},{56,48},{64,56},{72,6... | collective-permute-start | bytes 1474568 | tf_op jit(solution)/shard_map/ppermute | solution.py:16
  28.4 0.7 copy-start.2
  180.9 14.1 %collective-permute-start.1 = (f32[5,4,48,128]{3,2,1,0:T(8,128)S(1)}, f32[5,4,48,128]{3,2,1,0:T(8,128)S(1)}, u32[]{:S(2)}, u32[]{:S(2)}) collective-permute-start(f32[5,4,48,128]{3,2,1,0:T(8,128)S(1)} %slice.209), channel_id=1, source_target_pairs={{504,0},{0,8},{8,16},{16,24},{24,32},{32,40},{40,48},{48,56},{56,6... | collective-permute-start | bytes 1474568 | tf_op jit(solution)/shard_map/ppermute | solution.py:16
  195.2 1.4 copy-start
  196.9 11.9 %collective-permute-start.2 = (f32[3,4,48,128]{3,2,1,0:T(8,128)S(1)}, f32[3,4,48,128]{3,2,1,0:T(8,128)S(1)}, u32[]{:S(2)}, u32[]{:S(2)}) collective-permute-start(f32[3,4,48,128]{3,2,1,0:T(8,128)S(1)} %get-tuple-element.17), channel_id=1, source_target_pairs={{0,8},{8,16},{16,24},{24,32},{32,40},{40,48},{48,56},{56,64},{64,7... | collective-permute-start | bytes 884744 | tf_op jit(solution)/shard_map/ppermute | solution.py:26
  198.9 11.8 %collective-permute-start.3 = (f32[3,4,48,128]{3,2,1,0:T(8,128)S(1)}, f32[3,4,48,128]{3,2,1,0:T(8,128)S(1)}, u32[]{:S(2)}, u32[]{:S(2)}) collective-permute-start(f32[3,4,48,128]{3,2,1,0:T(8,128)S(1)} %get-tuple-element.18), channel_id=1, source_target_pairs={{8,0},{16,8},{24,16},{32,24},{40,32},{48,40},{56,48},{64,56},{72,6... | collective-permute-start | bytes 884744 | tf_op jit(solution)/shard_map/ppermute | solution.py:29
  212.6 25.9 %collective-permute-start.6 = (f32[3,1,48,128]{3,2,1,0:T(8,128)S(1)}, f32[3,1,48,128]{3,2,1,0:T(8,128)S(1)}, u32[]{:S(2)}, u32[]{:S(2)}) collective-permute-start(f32[3,1,48,128]{3,2,1,0:T(8,128)S(1)} %get-tuple-element.15), channel_id=1, source_target_pairs={{8,0},{16,8},{24,16},{32,24},{40,32},{48,40},{56,48},{64,56},{72,6... | collective-permute-start | bytes 221192 | tf_op jit(solution)/shard_map/ppermute | solution.py:29
  220.3 18.2 %collective-permute-start.7 = (f32[3,1,48,128]{3,2,1,0:T(8,128)S(1)}, f32[3,1,48,128]{3,2,1,0:T(8,128)S(1)}, u32[]{:S(2)}, u32[]{:S(2)}) collective-permute-start(f32[3,1,48,128]{3,2,1,0:T(8,128)S(1)} %get-tuple-element.16), channel_id=1, source_target_pairs={{0,8},{8,16},{16,24},{24,32},{32,40},{40,48},{48,56},{56,64},{64,7... | collective-permute-start | bytes 221192 | tf_op jit(solution)/shard_map/ppermute | solution.py:26
  222.3 7.2 %collective-permute-start.4 = (f32[3,16,1,128]{3,2,1,0:T(1,128)S(1)}, f32[3,16,1,128]{3,2,1,0:T(1,128)S(1)}, u32[]{:S(2)}, u32[]{:S(2)}) collective-permute-start(f32[3,16,1,128]{3,2,1,0:T(1,128)S(1)} %get-tuple-element.9), channel_id=1, source_target_pairs={{1,0},{2,1},{3,2},{4,3},{5,4},{6,5},{7,6},{9,8},{10,9},{11,10},{12... | collective-permute-start | bytes 73736 | tf_op jit(solution)/shard_map/ppermute | solution.py:29
  226.7 11.7 %collective-permute-start.5 = (f32[3,16,1,128]{3,2,1,0:T(1,128)S(1)}, f32[3,16,1,128]{3,2,1,0:T(1,128)S(1)}, u32[]{:S(2)}, u32[]{:S(2)}) collective-permute-start(f32[3,16,1,128]{3,2,1,0:T(1,128)S(1)} %get-tuple-element.10), channel_id=1, source_target_pairs={{0,1},{1,2},{2,3},{3,4},{4,5},{5,6},{6,7},{8,9},{9,10},{10,11},{11... | collective-permute-start | bytes 73736 | tf_op jit(solution)/shard_map/ppermute | solution.py:26
Sparse Core Ops, SparseCore 0:
  28.6 148.2 all-gather.2
